TPU v7x, 32 devices: a whole 2x2x4 slice. The times are simulated.
32 devices in a mesh: group: 4 (over y, x), dom: 8 (over z, core).
Axes of the slice: x: 2, y: 2, z: 4, core: 2. Of those that a mesh axis runs over, the one named last changes fastest.
Arguments:
- pin_feats: bfloat16 [32768, 256], P(('group', 'dom')), may hold values from -6 to 6
- w_self: bfloat16 [256, 256], replicated, may hold values from -0.375 to 0.375
- w_edge: bfloat16 [4, 256, 256], replicated, may hold values from -0.375 to 0.375
- w_head: bfloat16 [256, 1024], replicated, may hold values from -0.375 to 0.375
- w_out: bfloat16 [1024], replicated, may hold values from -0.1875 to 0.1875
- send_rows: int32 [32, 512], P(('group', 'dom')), may hold values from 0 to 1023
- edge_src: int32 [32, 4, 1024], P(('group', 'dom')), may hold values from 0 to 1535
- edge_dst: int32 [32, 4, 1024], P(('group', 'dom')), may hold values from 0 to 1023
- pin_owner: int32 [32768, 1], P(('group', 'dom')), may hold values from 0 to 31; in each aligned block of 1024 rows (0 to 1023, 1024 to 2047, ...) at most 64 rows name the same one
- pin_net: int32 [32768], P(('group', 'dom')), may hold values from 0 to 255
- net_target: float32 [8192], P(('group', 'dom')), may hold values from -6 to 6
Outputs:
- prediction: float32 [8192], P(('group', 'dom'))
- grad_feats: bfloat16 [32768, 256], P(('group', 'dom'))
- grad_self: float32 [256, 256], replicated
- grad_edge: float32 [4, 256, 256], replicated
- grad_head: float32 [256, 1024], replicated
- grad_out: float32 [1024], replicated
Inputs may be any that keep to these rules, and one draw needn't show every extreme that they name: `pin_owner`: among the pins of one device at most 64 name one owner, and in every draw some device sends exactly 64 pins to some owner.
All inputs are finite; a program needn't handle non-finite values.
Results may differ from a plain program's by a relative error of at most 0.0094.
Values may be sent and summed in bfloat16 or wider, within the bound.
No kernel may reach another device: no remote copies, remote signals or barrier semaphores. Data moves between devices by JAX's collectives and lax.ppermute only.
A program may use at most 64 MiB of HBM per device.

v0:
```python
import math
import jax
import jax.numpy as jnp
from jax import lax
from jax.sharding import PartitionSpec as P

F32 = jnp.float32
BF16 = jnp.bfloat16


def extended(block, sides, width):
    for axis, dim in sides:
        count = lax.axis_size(axis)
        forward = [(i, i + 1) for i in range(count - 1)]
        backward = [(target, source) for source, target in forward]
        low = lax.ppermute(
            lax.slice_in_dim(block, block.shape[dim] - width, None, axis=dim), axis, forward
        )
        high = lax.ppermute(lax.slice_in_dim(block, 0, width, axis=dim), axis, backward)
        block = jnp.concatenate([low, block, high], axis=dim)
    return block


def silu_slope(values):
    sigma_val = jax.nn.sigmoid(values)
    return sigma_val * (1.0 + values * (1.0 - sigma_val))


def one_hot(index, count):
    return (index[..., None] == jnp.arange(count, dtype=index.dtype)).astype(BF16)


def split_dot(spec, left, right):
    return jnp.einsum(
        spec, left, right.astype(F32), precision=lax.Precision.HIGHEST, preferred_element_type=F32
    )


def on_device(
    pin_feats,
    w_self,
    w_edge,
    w_head,
    w_out,
    send_rows,
    edge_src,
    edge_dst,
    pin_owner,
    pin_net,
    net_target,
):
    pin_count, feat_width = pin_feats.shape
    send_list = send_rows[0]
    halo_span = send_list.shape[0] // 2
    send_hot = one_hot(send_list, pin_count)
    outgoing = jnp.dot(send_hot, pin_feats, preferred_element_type=F32).astype(BF16)
    padded = extended(outgoing, (("dom", 0),), halo_span)
    node_table = jnp.concatenate([pin_feats, padded[:halo_span], padded[3 * halo_span :]], 0)
    table_rows = node_table.shape[0]
    sources = edge_src[0]
    endpoints = edge_dst[0]
    src_hot = one_hot(sources, table_rows)
    dst_hot = one_hot(endpoints, pin_count)
    gathered = jnp.einsum("ter,rd->ted", src_hot, node_table, preferred_element_type=F32).astype(
        BF16
    )
    edge_in = jnp.einsum("tep,ted->tpd", dst_hot, gathered, preferred_element_type=F32)
    summed = split_dot("tpk,tkd->pd", edge_in, w_edge)
    degree = jnp.sum(dst_hot.astype(F32), axis=(0, 1))
    inverse = 1.0 / (1.0 + degree)
    preact = jnp.dot(pin_feats, w_self, preferred_element_type=F32) + summed * inverse[:, None]
    hidden = jax.nn.silu(preact).astype(BF16)
    groups = lax.axis_size("group")
    domains = lax.axis_size("dom")
    owners = groups * domains
    capacity = max(2, 2 * pin_count // owners)
    net_count = net_target.shape[0]
    owner_ids = pin_owner[:, 0]
    owner_hot = one_hot(owner_ids, owners)
    earlier = (
        jnp.arange(pin_count, dtype=jnp.int32)[None, :]
        < jnp.arange(pin_count, dtype=jnp.int32)[:, None]
    ).astype(BF16)
    before = jnp.dot(earlier, owner_hot, preferred_element_type=F32)
    slot_rank = jnp.sum(before * owner_hot.astype(F32), axis=1).astype(jnp.int32)
    pin_slot = owner_ids * capacity + slot_rank
    slot_hot = one_hot(pin_slot, owners * capacity)
    net_code = (pin_net + 1).astype(BF16)[:, None]
    slot_nets = (
        jnp.dot(slot_hot.T, net_code, preferred_element_type=F32)[:, 0].astype(jnp.int32) - 1
    )
    slot_nets_in = lax.all_to_all(
        slot_nets.reshape(owners, capacity),
        ("group", "dom"),
        split_axis=0,
        concat_axis=0,
        tiled=True,
    ).reshape(-1)
    outbound = jnp.dot(slot_hot.T, hidden, preferred_element_type=F32).astype(BF16)
    inbound = lax.all_to_all(
        outbound.reshape(owners, capacity, feat_width),
        ("group", "dom"),
        split_axis=0,
        concat_axis=0,
        tiled=True,
    ).reshape(-1, feat_width)
    net_hot = one_hot(slot_nets_in, net_count)
    pooled = jnp.einsum("sn,sd->nd", net_hot, inbound, preferred_element_type=F32)
    pooled_b = pooled.astype(BF16)
    head_pre = jnp.dot(pooled_b, w_head, preferred_element_type=F32)
    activated = jax.nn.silu(head_pre).astype(BF16)
    predicted = jnp.dot(activated, w_out, preferred_element_type=F32)
    misfit = predicted - net_target
    head_grad = (misfit[:, None] * w_out.astype(F32)[None, :] * silu_slope(head_pre)).astype(BF16)
    head_sum = jnp.einsum("nd,nh->dh", pooled_b, head_grad, preferred_element_type=F32)
    out_sum = jnp.dot(misfit, activated.astype(F32), precision=lax.Precision.HIGHEST)
    head_totals = lax.psum(jnp.concatenate([head_sum, out_sum[None, :]], 0), ("group", "dom"))
    net_grad = jnp.einsum("nh,dh->nd", head_grad, w_head, preferred_element_type=F32).astype(BF16)
    returned = jnp.dot(net_hot, net_grad, preferred_element_type=F32).astype(BF16)
    arrived = lax.all_to_all(
        returned.reshape(owners, capacity, feat_width),
        ("group", "dom"),
        split_axis=0,
        concat_axis=0,
        tiled=True,
    ).reshape(-1, feat_width)
    pin_grad = jnp.dot(slot_hot, arrived, preferred_element_type=F32)
    preact_grad = (pin_grad * silu_slope(preact)).astype(BF16)
    self_sum = jnp.einsum("pk,pd->kd", pin_feats, preact_grad, preferred_element_type=F32)
    agg_grad = (preact_grad.astype(F32) * inverse[:, None]).astype(BF16)
    edge_rows = jnp.einsum("tep,pd->ted", dst_hot, agg_grad, preferred_element_type=F32).astype(
        BF16
    )
    edge_sum = jnp.einsum("tek,ted->tkd", gathered, edge_rows, preferred_element_type=F32)
    row_in = jnp.einsum("ter,ted->trd", src_hot, edge_rows, preferred_element_type=F32)
    table_grad = split_dot("trd,tkd->rk", row_in, w_edge)
    local_grad = (
        jnp.einsum("pd,kd->pk", preact_grad, w_self, preferred_element_type=F32)
        + table_grad[:pin_count]
    )
    halo_grad = table_grad[pin_count:].astype(BF16)
    back_padded = extended(halo_grad, (("dom", 0),), halo_span)
    received = jnp.concatenate([back_padded[:halo_span], back_padded[3 * halo_span :]], 0)
    grad_feats = (
        local_grad + jnp.einsum("sp,sd->pd", send_hot, received, preferred_element_type=F32)
    ).astype(BF16)
    self_sum, edge_sum, head_totals = lax.optimization_barrier((self_sum, edge_sum, head_totals))
    tail_totals = lax.psum((self_sum, edge_sum), ("group", "dom"))
    grad_scale = 1.0 / math.sqrt(pin_count * owners)
    return (
        predicted,
        grad_feats,
        tail_totals[0] * grad_scale,
        tail_totals[1] * grad_scale,
        head_totals[:feat_width] * grad_scale,
        head_totals[feat_width] * grad_scale,
    )


def solution(mesh):
    in_specs = (
        P(("group", "dom"), None),
        P(),
        P(),
        P(),
        P(),
        P(("group", "dom"), None),
        P(("group", "dom"), None, None),
        P(("group", "dom"), None, None),
        P(("group", "dom"), None),
        P(("group", "dom")),
        P(("group", "dom")),
    )
    out_specs = (P(("group", "dom")), P(("group", "dom"), None), P(), P(), P(), P())
    return jax.shard_map(
        on_device, mesh=mesh, in_specs=in_specs, out_specs=out_specs, check_vma=False
    )
```

profile of v0, /device:TPU:0, one launch (start us, length us, event | category | flops | bytes accessed | tf_op | source)
XLA Modules:
  0.0 383.9 jit_solution(4948331850442410509)
XLA Ops:
  7.2 0.0 copy-start
  7.2 0.7 add_convert_fusion
  7.9 1.3 fusion.31
  9.2 0.0 copy-start.2
  9.3 0.0 copy-start.14
  9.3 0.7 multiply_add_fusion
  10.0 1.5 fusion.11
  11.5 0.7 sub.16
  12.2 7.3 %all-to-all-start = ((s32[32,1,64]{2,1,0:T(1,128)}), s32[32,1,64]{2,1,0:T(1,128)S(1)}, u32[]{:S(2)}, u32[]{:S(2)}) async-start(s32[32,1,64]{2,1,0:T(1,128)} %sub.16), calls=%async_computation | async-start | bytes 32768 | tf_op jit(solution)/shard_map/all_to_all | solution.py:92
  19.5 0.5 fusion.28
  20.1 2.2 collective-permute-start
  22.2 1.3 collective-permute-start.1
  23.5 1.9 convert_reduce_fusion
  25.5 0.3 fusion.55
  25.8 0.0 collective-permute-done
  25.8 0.8 collective-permute-done.1
  26.6 4.8 %fusion.20 = bf16[4,1024,256]{2,1,0:T(8,128)(2,1)S(1)} fusion(s32[4,1024]{1,0:T(4,128)S(1)} %bitcast.74, bf16[256,256]{1,0:T(8,128)(2,1)S(1)} %collective-permute-done.1, bf16[256,256]{1,0:T(8,128)(2,1)S(1)} %collective-permute-done, bf16[1024,256]{1,0:T(8,128)(2,1)S(1)} %copy-done.2), kind=kOutput, calls=%fused_computation.29 | convolution fusion | flops 3230924800 | bytes 2899968 | tf_op jit(solution)/shard_map/ter,rd->ted/dot_general | solution.py:64
  31.5 0.0 copy-start.1
  31.5 5.8 %fusion.4 = f32[4,1024,256]{2,1,0:T(8,128)S(1)} fusion(bf16[4,1024,256]{2,1,0:T(8,128)(2,1)S(1)} %fusion.20, s32[4,1024]{1,0:T(4,128)S(1)} %bitcast.72), kind=kOutput, calls=%fused_computation.7 | convolution fusion | flops 2151677952 | bytes 6307840 | tf_op jit(solution)/shard_map/tep,ted->tpd/dot_general | solution.py:67
  37.2 2.1 fusion.24
  39.3 0.0 copy-start.7
  39.3 1.0 copy-done.7
  40.3 3.5 fusion.16
  43.8 0.0 all-to-all-done
  43.8 7.9 %all-to-all-start.1 = ((bf16[32,64,256]{2,1,0:T(8,128)(2,1)}), bf16[32,64,256]{2,1,0:T(8,128)(2,1)}, u32[]{:S(2)}, u32[]{:S(2)}) async-start(bf16[32,64,256]{2,1,0:T(8,128)(2,1)} %bitcast.60), calls=%async_computation.1 | async-start | bytes 2097152 | tf_op jit(solution)/shard_map/all_to_all | solution.py:100
  51.8 0.5 broadcast.42
  52.3 0.7 reduce.3
  53.0 0.1 eq.98
  53.0 26.2 %all-to-all-done.1 = bf16[32,64,256]{2,1,0:T(8,128)(2,1)} async-done(((bf16[32,64,256]{2,1,0:T(8,128)(2,1)}), bf16[32,64,256]{2,1,0:T(8,128)(2,1)}, u32[]{:S(2)}, u32[]{:S(2)}) %all-to-all-start.1) | async-done | bytes 1048608 | tf_op jit(solution)/shard_map/all_to_all | solution.py:100
  79.3 2.3 fusion.29
  81.6 0.0 copy-start.11
  81.6 0.4 multiply_convert_fusion.2
  82.1 0.8 copy-done.4
  82.8 0.2 fusion.56
  83.1 1.2 multiply_convert_fusion.1
  84.3 3.0 convolution_convert_fusion
  87.3 3.4 all-to-all-start.2
  90.7 0.0 all-reduce.4.cloned.1.call-start
  90.8 1.4 fusion.59
  92.1 1.4 fusion.58
  93.5 1.2 pad_maximum_fusion
  94.7 0.0 all-reduce.4.cloned.1.call-update
  94.7 0.0 all-reduce.6.cloned.1.call-start
  94.8 26.5 %all-to-all-done.2 = bf16[32,64,256]{2,1,0:T(8,128)(2,1)} async-done(((bf16[32,64,256]{2,1,0:T(8,128)(2,1)}), bf16[32,64,256]{2,1,0:T(8,128)(2,1)}, u32[]{:S(2)}, u32[]{:S(2)}) %all-to-all-start.2) | async-done | bytes 1048608 | tf_op jit(solution)/shard_map/all_to_all | solution.py:120
  121.2 3.3 fusion.26
  124.6 0.0 copy-start.5
  124.6 3.3 fusion.21
  127.9 0.0 copy-start.3
  127.9 9.3 %fusion = f32[4,1536,256]{2,1,0:T(8,128)} fusion(bf16[4,1024,256]{2,1,0:T(8,128)(2,1)S(1)} %fusion.21, s32[4,1024]{1,0:T(4,128)S(1)} %bitcast.75), kind=kOutput, calls=%fused_computation.1 | convolution fusion | flops 3227516928 | bytes 8404992 | tf_op jit(solution)/shard_map/ter,ted->trd/dot_general | solution.py:135
  137.2 1.0 convolution_bitcast_fusion.2
  138.3 1.9 fusion.57
  140.2 89.8 %all-reduce.4.cloned.1.call-done = f32[257,1024]{1,0:T(8,128)} async-done(((f32[257,1024]{1,0:T(8,128)}), f32[257,1024]{1,0:T(8,128)}) %all-reduce.4.cloned.1.call-update) | async-done | bytes 1052688 | tf_op jit(solution)/shard_map/psum | solution.py:117
  229.9 5.1 %fusion.54 = (bf16[1536,256]{1,0:T(8,128)(2,1)S(1)}, f32[1536,256]{1,0:T(8,128)S(1)}) fusion(f32[4,1536,256]{2,1,0:T(8,128)} %fusion, bf16[4,256,256]{2,1,0:T(8,128)(2,1)S(1)} %copy-done.1), kind=kOutput, calls=%fused_computation.83 | convolution fusion | flops 4832231424 | bytes 9175040 | tf_op jit(solution)/shard_map/trd,tkd->rk/dot_general | solution.py:34
  235.1 2.1 collective-permute-start.2
  237.2 1.3 collective-permute-start.3
  238.5 0.3 convolution_add_fusion
  238.8 0.0 all-reduce.6.cloned.1.call-update
  238.9 2.3 slice_multiply_fusion
  241.2 1.4 slice_multiply_fusion.1
  242.6 1.6 fusion.27
  244.2 128.8 %all-reduce.6.cloned.1.call-done = (f32[256,256]{0,1:T(8,128)}, f32[4,256,256]{2,1,0:T(8,128)}) async-done(((f32[256,256]{0,1:T(8,128)}, f32[4,256,256]{2,1,0:T(8,128)}), (f32[256,256]{0,1:T(8,128)}, f32[4,256,256]{2,1,0:T(8,128)})) %all-reduce.6.cloned.1.call-update) | async-done | bytes 1310736 | tf_op jit(solution)/shard_map/psum | solution.py:148
  373.0 1.0 broadcast_multiply_fusion.1
  373.9 0.8 copy.18
  374.8 2.3 broadcast_multiply_fusion
  (31 shorter events, 0.1 us)
Async XLA Ops:
  7.2 74.4 %copy-start = (bf16[256,1024]{1,0:T(8,128)(2,1)S(1)}, bf16[256,1024]{1,0:T(8,128)(2,1)}, u32[]{:S(2)}) copy-start(bf16[256,1024]{1,0:T(8,128)(2,1)} %param.14) | copy-start | bytes 1572868
  9.2 10.3 %copy-start.2 = (bf16[1024,256]{1,0:T(8,128)(2,1)S(1)}, bf16[1024,256]{1,0:T(8,128)(2,1)}, u32[]{:S(2)}) copy-start(bf16[1024,256]{1,0:T(8,128)(2,1)} %param.11) | copy-start | bytes 1572868
  9.3 10.3 %copy-start.14 = (s32[1,512]{1,0:T(1,128)S(1)}, s32[1,512]{1,0:T(1,128)}, u32[]{:S(2)}) copy-start(s32[1,512]{1,0:T(1,128)} %param.16) | copy-start | bytes 6148
  10.0 13.5 %copy-start.12 = (s32[1,4,1024]{2,1,0:T(4,128)S(1)}, s32[1,4,1024]{2,1,0:T(4,128)}, u32[]{:S(2)}) copy-start(s32[1,4,1024]{2,1,0:T(4,128)} %param.18) | copy-start | bytes 49156
  10.0 15.5 %copy-start.8 = (bf16[256,256]{1,0:T(8,128)(2,1)S(1)}, bf16[256,256]{1,0:T(8,128)(2,1)}, u32[]{:S(2)}) copy-start(bf16[256,256]{1,0:T(8,128)(2,1)} %param.12) | copy-start | bytes 393220
  11.5 15.1 %copy-start.13 = (s32[1,4,1024]{2,1,0:T(4,128)S(1)}, s32[1,4,1024]{2,1,0:T(4,128)}, u32[]{:S(2)}) copy-start(s32[1,4,1024]{2,1,0:T(4,128)} %param.17) | copy-start | bytes 49156
  12.2 31.6 %all-to-all-start = ((s32[32,1,64]{2,1,0:T(1,128)}), s32[32,1,64]{2,1,0:T(1,128)S(1)}, u32[]{:S(2)}, u32[]{:S(2)}) async-start(s32[32,1,64]{2,1,0:T(1,128)} %sub.16), calls=%async_computation | async-start | bytes 32768 | tf_op jit(solution)/shard_map/all_to_all | solution.py:92
  20.1 5.8 %collective-permute-start = (bf16[256,256]{1,0:T(8,128)(2,1)S(1)}, bf16[256,256]{1,0:T(8,128)(2,1)S(1)}, u32[]{:S(2)}, u32[]{:S(2)}) collective-permute-start(bf16[256,256]{1,0:T(8,128)(2,1)S(1)} %get-tuple-element.22), channel_id=1, source_target_pairs={{0,1},{1,2},{2,3},{3,4},{4,5},{5,6},{6,7},{8,9},{9,10},{10,11},{11... | collective-permute-start | bytes 393224 | tf_op jit(solution)/shard_map/ppermute | solution.py:16
  22.2 4.4 %collective-permute-start.1 = (bf16[256,256]{1,0:T(8,128)(2,1)S(1)}, bf16[256,256]{1,0:T(8,128)(2,1)S(1)}, u32[]{:S(2)}, u32[]{:S(2)}) collective-permute-start(bf16[256,256]{1,0:T(8,128)(2,1)S(1)} %get-tuple-element.23), channel_id=1, source_target_pairs={{1,0},{2,1},{3,2},{4,3},{5,4},{6,5},{7,6},{9,8},{10,9},{11,10},{12... | collective-permute-start | bytes 393224 | tf_op jit(solution)/shard_map/ppermute | solution.py:19
  31.5 5.8 %copy-start.1 = (bf16[4,256,256]{2,1,0:T(8,128)(2,1)S(1)}, bf16[4,256,256]{2,1,0:T(8,128)(2,1)}, u32[]{:S(2)}) copy-start(bf16[4,256,256]{2,1,0:T(8,128)(2,1)} %param.13) | copy-start | bytes 1572868
  39.3 1.0 copy-start.7
  43.8 7.9 %copy-start.9 = (bf16[1024]{0:T(1024)(128)(2,1)S(1)}, bf16[1024]{0:T(1024)(128)(2,1)}, u32[]{:S(2)}) copy-start(bf16[1024]{0:T(1024)(128)(2,1)} %param.15) | copy-start | bytes 6148
  43.8 35.5 %all-to-all-start.1 = ((bf16[32,64,256]{2,1,0:T(8,128)(2,1)}), bf16[32,64,256]{2,1,0:T(8,128)(2,1)}, u32[]{:S(2)}, u32[]{:S(2)}) async-start(bf16[32,64,256]{2,1,0:T(8,128)(2,1)} %bitcast.60), calls=%async_computation.1 | async-start | bytes 2097152 | tf_op jit(solution)/shard_map/all_to_all | solution.py:100
  81.6 1.5 copy-start.11
  82.0 0.8 copy-start.4
  83.1 4.2 %copy-start.10 = (f32[1,256]{1,0:T(1,128)}, f32[1,256]{1,0:T(1,128)S(1)}, u32[]{:S(2)}) copy-start(f32[1,256]{1,0:T(1,128)S(1)} %fusion.56) | copy-start | bytes 3076
  87.3 33.9 %all-to-all-start.2 = ((bf16[32,64,256]{2,1,0:T(8,128)(2,1)}), bf16[32,64,256]{2,1,0:T(8,128)(2,1)}, u32[]{:S(2)}, u32[]{:S(2)}) async-start(bf16[32,64,256]{2,1,0:T(8,128)(2,1)} %bitcast.59), calls=%async_computation.2 | async-start | bytes 2097152 | tf_op jit(solution)/shard_map/all_to_all | solution.py:120
  90.7 139.2 %all-reduce.4.cloned.1.call-start = ((), (), s32[]{:S(2)}) async-start(), calls=%async_computation.3 | async-start | bytes 2162688 | tf_op jit(solution)/shard_map/psum | solution.py:117
  94.7 278.2 %all-reduce.6.cloned.1.call-start = ((), (), s32[]{:S(2)}) async-start(), calls=%async_computation.4 | async-start | bytes 2621440 | tf_op jit(solution)/shard_map/psum | solution.py:148
  124.6 12.7 %copy-start.5 = (bf16[1024,256]{1,0:T(8,128)(2,1)}, bf16[1024,256]{1,0:T(8,128)(2,1)S(1)}, u32[]{:S(2)}) copy-start(bf16[1024,256]{1,0:T(8,128)(2,1)S(1)} %fusion.26) | copy-start | bytes 1572868
  127.9 9.4 %copy-start.3 = (bf16[1024,256]{1,0:T(8,128)(2,1)S(1)}, bf16[1024,256]{1,0:T(8,128)(2,1)}, u32[]{:S(2)}) copy-start(bf16[1024,256]{1,0:T(8,128)(2,1)} %param.11) | copy-start | bytes 1572868
  140.2 98.3 %copy-start.6 = (bf16[1024,256]{1,0:T(8,128)(2,1)S(1)}, bf16[1024,256]{1,0:T(8,128)(2,1)}, u32[]{:S(2)}) copy-start(bf16[1024,256]{1,0:T(8,128)(2,1)} %copy-done.5) | copy-start | bytes 1572868
  235.1 7.5 %collective-permute-start.2 = (bf16[256,256]{1,0:T(8,128)(2,1)S(1)}, bf16[256,256]{1,0:T(8,128)(2,1)S(1)}, u32[]{:S(2)}, u32[]{:S(2)}) collective-permute-start(bf16[256,256]{1,0:T(8,128)(2,1)S(1)} %get-tuple-element.20), channel_id=1, source_target_pairs={{0,1},{1,2},{2,3},{3,4},{4,5},{5,6},{6,7},{8,9},{9,10},{10,11},{11... | collective-permute-start | bytes 393224 | tf_op jit(solution)/shard_map/ppermute | solution.py:16
  237.2 5.4 %collective-permute-start.3 = (bf16[256,256]{1,0:T(8,128)(2,1)S(1)}, bf16[256,256]{1,0:T(8,128)(2,1)S(1)}, u32[]{:S(2)}, u32[]{:S(2)}) collective-permute-start(bf16[256,256]{1,0:T(8,128)(2,1)S(1)} %get-tuple-element.21), channel_id=1, source_target_pairs={{1,0},{2,1},{3,2},{4,3},{5,4},{6,5},{7,6},{9,8},{10,9},{11,10},{12... | collective-permute-start | bytes 393224 | tf_op jit(solution)/shard_map/ppermute | solution.py:19
Sparse Core Ops, SparseCore 0:
  97.0 132.9 all-reduce.3
  239.0 133.9 all-reduce.5
where the time goes:
time: 385 us; the launch traced here: 384 us
  waiting for transfers between devices  272 us (71%)
  matrix products  54.4 us (14%)
  starting transfers between devices  25.5 us (7%)
  between operations  14.4 us (4%)
  other arithmetic  13.6 us (4%)
  local copies, waits for them, and re-layouts  3.99 us (1%)
    psum x1, waiting for transfers between devices, on_device(): tail_totals = lax.psum((self_sum, edge_sum), ('group', 'dom'))  129 us
    psum x1, waiting for transfers between devices, on_device(): lax.psum(jnp.concatenate([head_sum, out_sum[None, :]], 0), ('group', 'dom'))  89.8 us
    all_to_all x1, waiting for transfers between devices, on_device(): lax.all_to_all(returned.reshape(owners, capacity, feat_width), ('group',...  26.5 us
    all_to_all x1, waiting for transfers between devices, on_device(): lax.all_to_all(outbound.reshape(owners, capacity, feat_width), ('group',...  26.2 us
    dot_general x1, matrix products, on_device(): jnp.einsum('ter,ted->trd', src_hot, edge_rows, preferred_element_type=F32)  9.33 us
    all_to_all x1, starting transfers between devices, on_device(): lax.all_to_all(outbound.reshape(owners, capacity, feat_width), ('group',...  7.91 us
  transfers between devices with their start and end apart: 9, of which 5 were waited for; matrix products, arithmetic and copies ran while one was open for 13% of the time, Pallas kernels for 0%

commit v1 on v0

--- a/solution.py
+++ b/solution.py
@@ -145,7 +145,9 @@
         local_grad + jnp.einsum("sp,sd->pd", send_hot, received, preferred_element_type=F32)
     ).astype(BF16)
     self_sum, edge_sum, head_totals = lax.optimization_barrier((self_sum, edge_sum, head_totals))
-    tail_totals = lax.psum((self_sum, edge_sum), ("group", "dom"))
+    tail_totals = (self_sum, edge_sum)
+    for over in ("dom", "group"):
+        tail_totals = lax.psum(tail_totals, over)
     grad_scale = 1.0 / math.sqrt(pin_count * owners)
     return (
         predicted,

time: 385 us -> 364 us (0.945)
  waiting for transfers between devices: 272 us -> 253 us
    psum x1 -> x2, waiting for transfers between devices: 129 us -> 99.6 us  [on_device(): tail_totals = lax.psum(tail_totals, over)]
    psum x1, waiting for transfers between devices: 89.8 us -> 98.7 us  [on_device(): lax.psum(jnp.concatenate([head_sum, out_sum[None, :]], 0), ('group', 'dom'))]
  transfers between devices with their start and end apart: 9 -> 10, of which waited for: 5 -> 7; matrix products, arithmetic and copies ran while one was open for 13% -> 15% of each run, Pallas kernels for 0% -> 0%
where the time goes in v1:
time: 364 us; the launch traced here: 363 us
  waiting for transfers between devices  253 us (70%)
  matrix products  55.9 us (15%)
  starting transfers between devices  25.1 us (7%)
  between operations  14.2 us (4%)
  other arithmetic  11.5 us (3%)
  local copies, waits for them, and re-layouts  4.13 us (1%)
    psum x2, waiting for transfers between devices, on_device(): tail_totals = lax.psum(tail_totals, over)  99.6 us
    psum x1, waiting for transfers between devices, on_device(): lax.psum(jnp.concatenate([head_sum, out_sum[None, :]], 0), ('group', 'dom'))  98.7 us
    all_to_all x1, waiting for transfers between devices, on_device(): lax.all_to_all(returned.reshape(owners, capacity, feat_width), ('group',...  26.6 us
    all_to_all x1, waiting for transfers between devices, on_device(): lax.all_to_all(outbound.reshape(owners, capacity, feat_width), ('group',...  26.2 us
    dot_general x1, matrix products, on_device(): jnp.einsum('ter,ted->trd', src_hot, edge_rows, preferred_element_type=F32)  10.5 us
    all_to_all x1, starting transfers between devices, on_device(): lax.all_to_all(outbound.reshape(owners, capacity, feat_width), ('group',...  7.91 us
    all_to_all x1, starting transfers between devices, on_device(): lax.all_to_all(slot_nets.reshape(owners, capacity), ('group', 'dom'), spl...  7.3 us
    dot_general x2, matrix products, split_dot(): jnp.einsum(spec, left, right.astype(F32), precision=lax.Precision.HIGHEST...  7.29 us
  transfers between devices with their start and end apart: 10, of which 7 were waited for; matrix products, arithmetic and copies ran while one was open for 15% of the time, Pallas kernels for 0%

profile of v1, /device:TPU:0, one launch (start us, length us, event | category | flops | bytes accessed | tf_op | source)
XLA Modules:
  0.0 363.2 jit_solution(11657426355957896693)
XLA Ops:
  7.2 0.0 copy-start
  7.2 0.7 add_convert_fusion
  7.9 1.3 fusion.31
  9.2 0.0 copy-start.3
  9.3 0.0 copy-start.16
  9.3 0.7 multiply_add_fusion
  10.0 1.5 fusion.11
  11.5 0.7 sub.16
  12.2 7.3 %all-to-all-start = ((s32[32,1,64]{2,1,0:T(1,128)}), s32[32,1,64]{2,1,0:T(1,128)S(1)}, u32[]{:S(2)}, u32[]{:S(2)}) async-start(s32[32,1,64]{2,1,0:T(1,128)} %sub.16), calls=%async_computation | async-start | bytes 32768 | tf_op jit(solution)/shard_map/all_to_all | solution.py:92
  19.5 0.5 fusion.28
  20.1 2.2 collective-permute-start
  22.2 1.3 collective-permute-start.1
  23.5 1.9 convert_reduce_fusion
  25.5 0.3 fusion.55
  25.8 0.8 collective-permute-done.1
  26.6 4.8 %fusion.20 = bf16[4,1024,256]{2,1,0:T(8,128)(2,1)S(1)} fusion(s32[4,1024]{1,0:T(4,128)S(1)} %bitcast.74, bf16[256,256]{1,0:T(8,128)(2,1)S(1)} %collective-permute-done.1, bf16[256,256]{1,0:T(8,128)(2,1)S(1)} %collective-permute-done, bf16[1024,256]{1,0:T(8,128)(2,1)S(1)} %copy-done.3), kind=kOutput, calls=%fused_computation.29 | convolution fusion | flops 3230924800 | bytes 2899968 | tf_op jit(solution)/shard_map/ter,rd->ted/dot_general | solution.py:64
  31.5 5.8 %fusion.4 = f32[4,1024,256]{2,1,0:T(8,128)S(1)} fusion(bf16[4,1024,256]{2,1,0:T(8,128)(2,1)S(1)} %fusion.20, s32[4,1024]{1,0:T(4,128)S(1)} %bitcast.72), kind=kOutput, calls=%fused_computation.7 | convolution fusion | flops 2151677952 | bytes 6307840 | tf_op jit(solution)/shard_map/tep,ted->tpd/dot_general | solution.py:67
  37.2 2.1 fusion.24
  39.3 0.0 copy-start.8
  39.3 1.0 copy-done.8
  40.3 3.5 fusion.16
  43.8 7.9 %all-to-all-start.1 = ((bf16[32,64,256]{2,1,0:T(8,128)(2,1)}), bf16[32,64,256]{2,1,0:T(8,128)(2,1)}, u32[]{:S(2)}, u32[]{:S(2)}) async-start(bf16[32,64,256]{2,1,0:T(8,128)(2,1)} %bitcast.60), calls=%async_computation.1 | async-start | bytes 2097152 | tf_op jit(solution)/shard_map/all_to_all | solution.py:100
  51.8 0.5 broadcast.42
  52.3 0.7 reduce.3
  53.0 0.1 eq.98
  53.0 26.2 %all-to-all-done.1 = bf16[32,64,256]{2,1,0:T(8,128)(2,1)} async-done(((bf16[32,64,256]{2,1,0:T(8,128)(2,1)}), bf16[32,64,256]{2,1,0:T(8,128)(2,1)}, u32[]{:S(2)}, u32[]{:S(2)}) %all-to-all-start.1) | async-done | bytes 1048608 | tf_op jit(solution)/shard_map/all_to_all | solution.py:100
  79.3 2.3 fusion.29
  81.6 0.0 copy-start.13
  81.6 0.4 multiply_convert_fusion.2
  82.1 0.8 copy-done.5
  82.8 0.2 fusion.56
  83.1 1.2 multiply_convert_fusion.1
  84.3 3.0 convolution_convert_fusion
  87.3 3.4 all-to-all-start.2
  90.7 0.0 all-reduce.6.cloned.1.call-start
  90.8 1.4 fusion.59
  92.1 1.4 fusion.58
  93.5 1.1 pad_maximum_fusion
  94.6 0.0 all-reduce.6.cloned.1.call-update
  94.7 0.0 all-reduce.8.cloned.1.call-start
  94.7 26.6 %all-to-all-done.2 = bf16[32,64,256]{2,1,0:T(8,128)(2,1)} async-done(((bf16[32,64,256]{2,1,0:T(8,128)(2,1)}), bf16[32,64,256]{2,1,0:T(8,128)(2,1)}, u32[]{:S(2)}, u32[]{:S(2)}) %all-to-all-start.2) | async-done | bytes 1048608 | tf_op jit(solution)/shard_map/all_to_all | solution.py:120
  121.3 3.3 fusion.26
  124.6 3.3 fusion.21
  127.9 1.3 convolution_bitcast_fusion.2
  129.2 0.1 copy-done.2
  129.4 1.9 fusion.57
  131.2 98.7 %all-reduce.6.cloned.1.call-done = f32[257,1024]{1,0:T(8,128)} async-done(((f32[257,1024]{1,0:T(8,128)}), f32[257,1024]{1,0:T(8,128)}) %all-reduce.6.cloned.1.call-update) | async-done | bytes 1052688 | tf_op jit(solution)/shard_map/psum | solution.py:117
  229.9 0.0 all-reduce.8.cloned.1.call-update
  230.0 0.3 all-reduce.10.cloned.1.call-start
  230.2 10.5 %fusion = f32[4,1536,256]{2,1,0:T(8,128)} fusion(bf16[4,1024,256]{2,1,0:T(8,128)(2,1)} %copy-done.2, s32[4,1024]{1,0:T(4,128)S(1)} %bitcast.75), kind=kOutput, calls=%fused_computation.1 | convolution fusion | flops 3227516928 | bytes 8404992 | tf_op jit(solution)/shard_map/ter,ted->trd/dot_general | solution.py:135
  240.7 52.8 %all-reduce.8.cloned.1.call-done = (f32[256,256]{0,1:T(8,128)}, f32[4,256,256]{2,1,0:T(8,128)}) async-done(((f32[256,256]{0,1:T(8,128)}, f32[4,256,256]{2,1,0:T(8,128)}), (f32[256,256]{0,1:T(8,128)}, f32[4,256,256]{2,1,0:T(8,128)})) %all-reduce.8.cloned.1.call-update) | async-done | bytes 1310736 | tf_op jit(solution)/shard_map/psum | solution.py:150
  293.5 0.0 all-reduce.10.cloned.1.call-update
  293.5 5.2 %fusion.54 = (bf16[1536,256]{1,0:T(8,128)(2,1)S(1)}, f32[1536,256]{1,0:T(8,128)S(1)}) fusion(f32[4,1536,256]{2,1,0:T(8,128)} %fusion, bf16[4,256,256]{2,1,0:T(8,128)(2,1)S(1)} %copy-done.1), kind=kOutput, calls=%fused_computation.83 | convolution fusion | flops 4832231424 | bytes 9175040 | tf_op jit(solution)/shard_map/trd,tkd->rk/dot_general | solution.py:34
  298.8 1.4 collective-permute-start.2
  300.2 1.3 collective-permute-start.3
  301.5 1.1 slice_multiply_fusion
  302.6 0.3 convolution_add_fusion
  303.0 0.6 slice_multiply_fusion.1
  303.6 0.6 collective-permute-done.3
  304.1 1.6 fusion.27
  305.8 46.8 %all-reduce.10.cloned.1.call-done = (f32[256,256]{0,1:T(8,128)}, f32[4,256,256]{2,1,0:T(8,128)}) async-done(((f32[256,256]{0,1:T(8,128)}, f32[4,256,256]{2,1,0:T(8,128)}), (f32[256,256]{0,1:T(8,128)}, f32[4,256,256]{2,1,0:T(8,128)})) %all-reduce.10.cloned.1.call-update) | async-done | bytes 1310736 | tf_op jit(solution)/shard_map/psum | solution.py:150
  352.6 1.0 broadcast_multiply_fusion.1
  353.6 0.8 copy.18
  354.4 2.3 broadcast_multiply_fusion
  (38 shorter events, 0.2 us)
Async XLA Ops:
  7.2 74.4 %copy-start = (bf16[256,1024]{1,0:T(8,128)(2,1)S(1)}, bf16[256,1024]{1,0:T(8,128)(2,1)}, u32[]{:S(2)}) copy-start(bf16[256,1024]{1,0:T(8,128)(2,1)} %param.14) | copy-start | bytes 1572868
  9.2 10.3 %copy-start.3 = (bf16[1024,256]{1,0:T(8,128)(2,1)S(1)}, bf16[1024,256]{1,0:T(8,128)(2,1)}, u32[]{:S(2)}) copy-start(bf16[1024,256]{1,0:T(8,128)(2,1)} %param.11) | copy-start | bytes 1572868
  9.3 10.3 %copy-start.16 = (s32[1,512]{1,0:T(1,128)S(1)}, s32[1,512]{1,0:T(1,128)}, u32[]{:S(2)}) copy-start(s32[1,512]{1,0:T(1,128)} %param.16) | copy-start | bytes 6148
  10.0 13.5 %copy-start.14 = (s32[1,4,1024]{2,1,0:T(4,128)S(1)}, s32[1,4,1024]{2,1,0:T(4,128)}, u32[]{:S(2)}) copy-start(s32[1,4,1024]{2,1,0:T(4,128)} %param.18) | copy-start | bytes 49156
  10.0 15.5 %copy-start.10 = (bf16[256,256]{1,0:T(8,128)(2,1)S(1)}, bf16[256,256]{1,0:T(8,128)(2,1)}, u32[]{:S(2)}) copy-start(bf16[256,256]{1,0:T(8,128)(2,1)} %param.12) | copy-start | bytes 393220
  11.5 15.1 %copy-start.15 = (s32[1,4,1024]{2,1,0:T(4,128)S(1)}, s32[1,4,1024]{2,1,0:T(4,128)}, u32[]{:S(2)}) copy-start(s32[1,4,1024]{2,1,0:T(4,128)} %param.17) | copy-start | bytes 49156
  12.2 31.6 %all-to-all-start = ((s32[32,1,64]{2,1,0:T(1,128)}), s32[32,1,64]{2,1,0:T(1,128)S(1)}, u32[]{:S(2)}, u32[]{:S(2)}) async-start(s32[32,1,64]{2,1,0:T(1,128)} %sub.16), calls=%async_computation | async-start | bytes 32768 | tf_op jit(solution)/shard_map/all_to_all | solution.py:92
  20.1 5.8 %collective-permute-start = (bf16[256,256]{1,0:T(8,128)(2,1)S(1)}, bf16[256,256]{1,0:T(8,128)(2,1)S(1)}, u32[]{:S(2)}, u32[]{:S(2)}) collective-permute-start(bf16[256,256]{1,0:T(8,128)(2,1)S(1)} %get-tuple-element.24), channel_id=1, source_target_pairs={{0,1},{1,2},{2,3},{3,4},{4,5},{5,6},{6,7},{8,9},{9,10},{10,11},{11... | collective-permute-start | bytes 393224 | tf_op jit(solution)/shard_map/ppermute | solution.py:16
  22.2 4.4 %collective-permute-start.1 = (bf16[256,256]{1,0:T(8,128)(2,1)S(1)}, bf16[256,256]{1,0:T(8,128)(2,1)S(1)}, u32[]{:S(2)}, u32[]{:S(2)}) collective-permute-start(bf16[256,256]{1,0:T(8,128)(2,1)S(1)} %get-tuple-element.25), channel_id=1, source_target_pairs={{1,0},{2,1},{3,2},{4,3},{5,4},{6,5},{7,6},{9,8},{10,9},{11,10},{12... | collective-permute-start | bytes 393224 | tf_op jit(solution)/shard_map/ppermute | solution.py:19
  31.5 5.8 %copy-start.1 = (bf16[4,256,256]{2,1,0:T(8,128)(2,1)S(1)}, bf16[4,256,256]{2,1,0:T(8,128)(2,1)}, u32[]{:S(2)}) copy-start(bf16[4,256,256]{2,1,0:T(8,128)(2,1)} %param.13) | copy-start | bytes 1572868
  39.3 1.0 copy-start.8
  43.8 7.9 %copy-start.11 = (bf16[1024]{0:T(1024)(128)(2,1)S(1)}, bf16[1024]{0:T(1024)(128)(2,1)}, u32[]{:S(2)}) copy-start(bf16[1024]{0:T(1024)(128)(2,1)} %param.15) | copy-start | bytes 6148
  43.8 35.5 %all-to-all-start.1 = ((bf16[32,64,256]{2,1,0:T(8,128)(2,1)}), bf16[32,64,256]{2,1,0:T(8,128)(2,1)}, u32[]{:S(2)}, u32[]{:S(2)}) async-start(bf16[32,64,256]{2,1,0:T(8,128)(2,1)} %bitcast.60), calls=%async_computation.1 | async-start | bytes 2097152 | tf_op jit(solution)/shard_map/all_to_all | solution.py:100
  81.6 1.5 copy-start.13
  82.0 0.8 copy-start.5
  83.1 4.2 %copy-start.12 = (f32[1,256]{1,0:T(1,128)}, f32[1,256]{1,0:T(1,128)S(1)}, u32[]{:S(2)}) copy-start(f32[1,256]{1,0:T(1,128)S(1)} %fusion.56) | copy-start | bytes 3076
  87.3 33.9 %all-to-all-start.2 = ((bf16[32,64,256]{2,1,0:T(8,128)(2,1)}), bf16[32,64,256]{2,1,0:T(8,128)(2,1)}, u32[]{:S(2)}, u32[]{:S(2)}) async-start(bf16[32,64,256]{2,1,0:T(8,128)(2,1)} %bitcast.59), calls=%async_computation.2 | async-start | bytes 2097152 | tf_op jit(solution)/shard_map/all_to_all | solution.py:120
  90.7 139.2 %all-reduce.6.cloned.1.call-start = ((), (), s32[]{:S(2)}) async-start(), calls=%async_computation.3 | async-start | bytes 2162688 | tf_op jit(solution)/shard_map/psum | solution.py:117
  94.7 198.9 %all-reduce.8.cloned.1.call-start = ((), (), s32[]{:S(2)}) async-start(), calls=%async_computation.4 | async-start | bytes 2621440 | tf_op jit(solution)/shard_map/psum | solution.py:150
  124.6 3.3 copy-start.6
  124.6 3.3 copy-start.4
  127.9 1.5 copy-start.2
  230.0 122.6 %all-reduce.10.cloned.1.call-start = ((), (), s32[]{:S(2)}) async-start(), calls=%async_computation.5 | async-start | bytes 2621440 | tf_op jit(solution)/shard_map/psum | solution.py:150
  293.5 8.0 %copy-start.9 = (f32[257,1024]{1,0:T(8,128)S(1)}, f32[257,1024]{1,0:T(8,128)}, u32[]{:S(2)}) copy-start(f32[257,1024]{1,0:T(8,128)} %all-reduce.6.cloned.1.call-done) | copy-start | bytes 3158020
  298.8 3.9 %copy-start.7 = (bf16[1024,256]{1,0:T(8,128)(2,1)S(1)}, bf16[1024,256]{1,0:T(8,128)(2,1)}, u32[]{:S(2)}) copy-start(bf16[1024,256]{1,0:T(8,128)(2,1)} %copy-done.6) | copy-start | bytes 1572868
  298.8 4.8 %collective-permute-start.2 = (bf16[256,256]{1,0:T(8,128)(2,1)S(1)}, bf16[256,256]{1,0:T(8,128)(2,1)S(1)}, u32[]{:S(2)}, u32[]{:S(2)}) collective-permute-start(bf16[256,256]{1,0:T(8,128)(2,1)S(1)} %get-tuple-element.22), channel_id=1, source_target_pairs={{0,1},{1,2},{2,3},{3,4},{4,5},{5,6},{6,7},{8,9},{9,10},{10,11},{11... | collective-permute-start | bytes 393224 | tf_op jit(solution)/shard_map/ppermute | solution.py:16
  300.2 3.9 %collective-permute-start.3 = (bf16[256,256]{1,0:T(8,128)(2,1)S(1)}, bf16[256,256]{1,0:T(8,128)(2,1)S(1)}, u32[]{:S(2)}, u32[]{:S(2)}) collective-permute-start(bf16[256,256]{1,0:T(8,128)(2,1)S(1)} %get-tuple-element.23), channel_id=1, source_target_pairs={{1,0},{2,1},{3,2},{4,3},{5,4},{6,5},{7,6},{9,8},{10,9},{11,10},{12... | collective-permute-start | bytes 393224 | tf_op jit(solution)/shard_map/ppermute | solution.py:19
Sparse Core Ops, SparseCore 0:
  97.0 132.9 all-reduce.5
  233.1 60.3 all-reduce.7
  296.9 55.6 all-reduce.9
